TPU v7x, 32 devices: a whole 2x2x4 slice. The times are simulated.
32 devices in a mesh: rep: 2 (over y), seq: 4 (over z), head: 4 (over x, core).
Axes of the slice: x: 2, y: 2, z: 4, core: 2. Of those that a mesh axis runs over, the one named last changes fastest.
Arguments:
- queries: bfloat16 [3072, 2560], P(('rep', 'seq'), 'head'), parts along dimension 0, may hold values from -16 to 16
- keys: bfloat16 [3072, 2560], P(('rep', 'seq'), 'head'), parts along dimension 0, may hold values from -6 to 6
- values: bfloat16 [3072, 2560], P(('rep', 'seq'), 'head'), parts along dimension 0, may hold values from -6 to 6
- out_weight: bfloat16 [2560, 5120], P('seq', 'head'), may hold values from -0.3125 to 0.3125
- neighbours: int32 [8, 27], P('rep'), parts along dimension 0, may hold values from -1 to 3, as said below
- clip_ids: int32 [3072], P(('rep', 'seq')), parts along dimension 0, may hold values from 0 to 1
Outputs:
- output: bfloat16 [3072, 5120], P(('rep', 'seq'), 'head'), parts along dimension 0
There are 2 independent parts, one for each index of `rep`. A program takes and returns all parts, laid end to end along the dimension named above; an argument that names none is the same for every part. Nothing has to cross between parts.
Inputs may be any that keep to these rules, and one draw needn't show every extreme that they name: `neighbours`: column 9 (a + 1) + 3 (b + 1) + (c + 1) of row s, for a, b, c each -1, 0 or 1, is either -1 or s + a * 4 * 7 + b * 7 + c; column 13 of row s is s.
All inputs are finite; a program needn't handle non-finite values.
Results may differ from a plain program's by a relative error of at most 0.0058.
Values may be sent and summed in bfloat16 or wider, within the bound.
No kernel may reach another device: no remote copies, remote signals or barrier semaphores. Data moves between devices by JAX's collectives and lax.ppermute only.
A program may use at most 192 MiB of HBM per device.

v0:
```python
import math
import jax
import jax.numpy as jnp
from jax import lax
from jax.sharding import PartitionSpec as P

HD = 128
TGH = 4
TGW = 7


def from_behind(value, axis, by):
    peers = lax.axis_size(axis)
    pairs = [(i, i + by) for i in range(peers) if 0 <= i + by < peers]
    return lax.ppermute(value, axis, pairs)


def chunk_bounds(size, unit=16, parts=4):
    units = size // unit
    bounds = []
    first = 0
    for index in range(parts):
        last = size if index == parts - 1 else first + units // parts * unit
        if last > first:
            bounds.append((first, last))
        first = last
    return bounds


def attend_head(query_head, key_head, value_head, allowed):
    scores = lax.dot_general(
        query_head, key_head, (((1,), (1,)), ((), ())), preferred_element_type=jnp.float32
    ) * (1.0 / math.sqrt(query_head.shape[1]))
    masked = jnp.where(allowed, scores, -1e30)
    highest = jnp.max(masked, axis=1, keepdims=True)
    raised = jnp.where(allowed, jnp.exp(masked - highest), 0.0)
    summed = jnp.sum(raised, axis=1, keepdims=True)
    weights = (raised / summed).astype(jnp.bfloat16)
    return jnp.dot(weights, value_head, preferred_element_type=jnp.float32).astype(jnp.bfloat16)


def on_device(queries, keys, values, out_weight, neighbours, clip_ids):
    tile_rows = queries.shape[0]
    feature_width = queries.shape[1]
    seq_count = lax.axis_size("seq")
    layer_tiles = TGH * TGW
    every_offset = set()
    for layer_step in (-1, 0, 1):
        for row_step in (-1, 0, 1):
            for col_step in (-1, 0, 1):
                every_offset.add(layer_step * layer_tiles + row_step * TGW + col_step)
    distances = [offset for offset in sorted(every_offset) if 0 < offset < seq_count]
    rep_position = lax.axis_index("rep")
    half_width = out_weight.shape[1] // 2
    block_rows = out_weight.shape[0]
    own_half = lax.dynamic_slice_in_dim(out_weight, rep_position * half_width, half_width, axis=1)
    row_chunks = chunk_bounds(block_rows)
    gathered = [
        lax.all_gather(own_half[first:last], "seq", axis=0, tiled=True)
        for first, last in row_chunks
    ]
    key_list = [keys]
    value_list = [values]
    clip_list = [clip_ids]
    offsets = [0]
    for distance in distances:
        below_keys, below_values, below_clips = from_behind(
            (keys, values, clip_ids), "seq", distance
        )
        above_keys, above_values, above_clips = from_behind(
            (keys, values, clip_ids), "seq", -distance
        )
        key_list += [below_keys, above_keys]
        value_list += [below_values, above_values]
        clip_list += [below_clips, above_clips]
        offsets += [distance, -distance]
    key_stack = jnp.stack(key_list)
    value_stack = jnp.stack(value_list)
    clip_stack = jnp.stack(clip_list)
    first_chunk, key_stack, value_stack, clip_stack = lax.optimization_barrier(
        (gathered[0], key_stack, value_stack, clip_stack)
    )
    crossed = [lax.ppermute(first_chunk, "rep", [(0, 1), (1, 0)])]
    blocks = key_stack.shape[0]
    position = lax.axis_index("seq")
    window_row = lax.dynamic_index_in_dim(neighbours, position, 0, keepdims=False)
    sources = position - jnp.asarray(offsets, dtype=jnp.int32)
    present = jnp.any(
        (window_row[None, :] == sources[:, None]) & (window_row[None, :] >= 0), axis=1
    )
    key_clips = clip_stack.reshape(blocks * tile_rows)
    allowed = jnp.repeat(present, tile_rows)[None, :] & (clip_ids[:, None] == key_clips[None, :])
    key_rows = key_stack.reshape(blocks * tile_rows, feature_width)
    value_rows = value_stack.reshape(blocks * tile_rows, feature_width)
    head_outputs = []
    for head_index in range(feature_width // HD):
        first_col = head_index * HD
        head_outputs.append(
            attend_head(
                queries[:, first_col : first_col + HD],
                key_rows[:, first_col : first_col + HD],
                value_rows[:, first_col : first_col + HD],
                allowed,
            )
        )
    attended = jnp.concatenate(head_outputs, axis=1)
    for index in range(1, len(gathered)):
        gathered[index], crossed[-1] = lax.optimization_barrier((gathered[index], crossed[-1]))
        crossed.append(lax.ppermute(gathered[index], "rep", [(0, 1), (1, 0)]))
    head_count = lax.axis_size("head")
    head_position = lax.axis_index("head")
    received = [attended]
    for shift in range(1, head_count):
        pairs = [(j, (j + shift) % head_count) for j in range(head_count)]
        received.append(lax.ppermute(attended, "head", pairs))
    ordered = []
    for group in range(head_count):
        block = received[0]
        for shift in range(1, head_count):
            block = jnp.where((head_position - shift) % head_count == group, received[shift], block)
        ordered.append(block)
    features = jnp.concatenate(ordered, axis=1)
    blocks = features.shape[1] // block_rows
    own_sum = None
    other_sum = None
    for (first, last), chunk, twin_chunk in zip(row_chunks, gathered, crossed):
        rows = features.reshape(tile_rows, blocks, block_rows)[:, :, first:last]
        rows = rows.reshape(tile_rows, blocks * (last - first))
        own_part = jnp.dot(rows, chunk, preferred_element_type=jnp.float32)
        other_part = jnp.dot(rows, twin_chunk, preferred_element_type=jnp.float32)
        own_sum = own_part if own_sum is None else own_sum + own_part
        other_sum = other_part if other_sum is None else other_sum + other_part
    own_out = own_sum.astype(jnp.bfloat16)
    other_out = other_sum.astype(jnp.bfloat16)
    return jnp.where(
        rep_position == 0,
        jnp.concatenate([own_out, other_out], axis=1),
        jnp.concatenate([other_out, own_out], axis=1),
    )


def solution(mesh):
    in_specs = (
        P(("rep", "seq"), "head"),
        P(("rep", "seq"), "head"),
        P(("rep", "seq"), "head"),
        P("seq", "head"),
        P("rep", None),
        P(("rep", "seq")),
    )
    out_specs = P(("rep", "seq"), "head")
    return jax.shard_map(
        on_device, mesh=mesh, in_specs=in_specs, out_specs=out_specs, check_vma=False
    )
```

profile of v0, /device:TPU:0, one launch (start us, length us, event | category | flops | bytes accessed | tf_op | source)
XLA Modules:
  0.0 180.5 jit_solution(5776254294343076778)
XLA Ops:
  0.0 4.9 %collective-permute-start = (bf16[384,640]{1,0:T(8,128)(2,1)}, bf16[384,640]{1,0:T(8,128)(2,1)S(1)}, u32[]{:S(2)}, u32[]{:S(2)}) collective-permute-start(bf16[384,640]{1,0:T(8,128)(2,1)} %param.8), channel_id=1, source_target_pairs={{0,4},{4,8},{8,12},{1,5},{5,9},{9,13},{2,6},{6,10},{10,14},{3,7},{... | collective-permute-start | bytes 1474568 | tf_op jit(solution)/shard_map/ppermute | solution.py:15
  5.0 1.3 collective-permute-start.1
  6.3 4.6 %collective-permute-start.2 = (bf16[384,640]{1,0:T(8,128)(2,1)}, bf16[384,640]{1,0:T(8,128)(2,1)S(1)}, u32[]{:S(2)}, u32[]{:S(2)}) collective-permute-start(bf16[384,640]{1,0:T(8,128)(2,1)} %param.9), channel_id=1, source_target_pairs={{0,4},{4,8},{8,12},{1,5},{5,9},{9,13},{2,6},{6,10},{10,14},{3,7},{... | collective-permute-start | bytes 1474568 | tf_op jit(solution)/shard_map/ppermute | solution.py:15
  10.8 1.3 collective-permute-start.3
  12.1 4.5 %collective-permute-start.4 = (s32[384]{0:T(512)}, s32[384]{0:T(512)S(1)}, u32[]{:S(2)}, u32[]{:S(2)}) collective-permute-start(s32[384]{0:T(512)} %param.12), channel_id=1, source_target_pairs={{0,4},{4,8},{8,12},{1,5},{5,9},{9,13},{2,6},{6,10},{10,14},{3,7},{... | collective-permute-start | bytes 4616 | tf_op jit(solution)/shard_map/ppermute | solution.py:15
  16.8 1.4 fusion.47
  18.1 27.4 %all_gather.12 = bf16[640,640]{1,0:T(8,128)(2,1)S(1)} all-gather(bf16[160,640]{1,0:T(8,128)(2,1)S(1)} %get-tuple-element.40), channel_id=1, replica_groups=mesh['rep'=2,'seq'=4,'head'=4] {'seq'}, dimensions={0}, use_global_device_ids=true | all-gather | bytes 1024000 | tf_op jit(solution)/shard_map/all_gather | solution.py:59
  45.6 18.1 %all_gather.13 = bf16[640,640]{1,0:T(8,128)(2,1)S(1)} all-gather(bf16[160,640]{1,0:T(8,128)(2,1)S(1)} %get-tuple-element.38), channel_id=1, replica_groups=mesh['rep'=2,'seq'=4,'head'=4] {'seq'}, dimensions={0}, use_global_device_ids=true | all-gather | bytes 1024000 | tf_op jit(solution)/shard_map/all_gather | solution.py:59
  64.0 1.3 collective-permute-start.5
  65.4 4.0 %collective-permute-done.5 = s32[384]{0:T(512)S(1)} collective-permute-done((s32[384]{0:T(512)S(1)}, s32[384]{0:T(512)S(1)}, u32[]{:S(2)}, u32[]{:S(2)}) %collective-permute-start.5) | collective-permute-done | bytes 1568 | tf_op jit(solution)/shard_map/ppermute | solution.py:15
  69.5 2.4 %pad_maximum_fusion.1 = bf16[3,384,640]{2,1,0:T(8,128)(2,1)} fusion(bf16[1,384,640]{2,1,0:T(8,128)(2,1)} %bitcast.4, bf16[1,384,640]{2,1,0:T(8,128)(2,1)S(1)} %bitcast.75, bf16[1,384,640]{2,1,0:T(8,128)(2,1)S(1)} %bitcast.72), kind=kLoop, calls=%fused_computation.27 | loop fusion | flops 1474560 | bytes 2949120 | tf_op jit(solution)/shard_map/stack | solution.py:77
  72.7 1.5 pad_maximum_fusion.2
  74.2 2.2 %fusion.51 = (f32[384]{0:T(512)S(1)}, f32[384,1152]{0,1:T(8,128)S(1)}) fusion(bf16[384,640]{1,0:T(8,128)(2,1)} %param.7, bf16[1152,640]{1,0:T(8,128)(2,1)} %bitcast.67, s32[1152]{0:T(1024)S(1)} %eq.89, s32[384]{0:T(512)S(1)} %copy-done.3, pred[1152]{0:T(1024)(128)(4,1)S(1)} %and.49), kind=kOutput, calls=%fused_computation.89 | convolution fusion | flops 115457664 | bytes 2171520 | tf_op jit(solution)/shard_map/dot_general | solution.py:31
  78.9 1.6 collective-permute-start.9
  80.5 2.2 %fusion.19 = (f32[384]{0:T(512)S(1)}, f32[384]{0:T(512)S(1)}, f32[384]{0:T(512)S(1)}, f32[384]{0:T(512)S(1)}, f32[384]{0:T(512)S(1)}) fusion(f32[384,1152]{0,1:T(8,128)S(1)} %get-tuple-element.43, f32[384]{0:T(512)S(1)} %get-tuple-element.42, s32[384]{0:T(512)S(1)} %copy-done.3, s32[1152]{0:T(1024)S(1)} %eq.89, pred[1152]{0:T(1024)(128)(4,1)S(1)} %and.49, ...), kind=kLoop, calls=%fused_computation.41 | loop fusion | flops 7518336 | bytes 8870016 | tf_op jit(solution)/shard_map/reduce_sum | solution.py:37
  83.7 0.9 fusion.21
  85.5 0.9 fusion.23
  87.4 1.6 collective-permute-start.7
  89.2 18.4 %all_gather.14 = bf16[640,640]{1,0:T(8,128)(2,1)S(1)} all-gather(bf16[160,640]{1,0:T(8,128)(2,1)S(1)} %get-tuple-element.39), channel_id=1, replica_groups=mesh['rep'=2,'seq'=4,'head'=4] {'seq'}, dimensions={0}, use_global_device_ids=true | all-gather | bytes 1024000 | tf_op jit(solution)/shard_map/all_gather | solution.py:59
  107.6 18.5 %all_gather.15 = bf16[640,640]{1,0:T(8,128)(2,1)S(1)} all-gather(bf16[160,640]{1,0:T(8,128)(2,1)S(1)} %get-tuple-element.41), channel_id=1, replica_groups=mesh['rep'=2,'seq'=4,'head'=4] {'seq'}, dimensions={0}, use_global_device_ids=true | all-gather | bytes 1024000 | tf_op jit(solution)/shard_map/all_gather | solution.py:59
  127.4 17.1 %collective-permute-done.10 = bf16[640,640]{1,0:T(8,128)(2,1)S(1)} collective-permute-done((bf16[640,640]{1,0:T(8,128)(2,1)S(1)}, bf16[640,640]{1,0:T(8,128)(2,1)S(1)}, u32[]{:S(2)}, u32[]{:S(2)}) %collective-permute-start.10) | collective-permute-done | bytes 819232 | tf_op jit(solution)/shard_map/ppermute | solution.py:109
  146.9 16.0 %collective-permute-done.11 = bf16[640,640]{1,0:T(8,128)(2,1)S(1)} collective-permute-done((bf16[640,640]{1,0:T(8,128)(2,1)S(1)}, bf16[640,640]{1,0:T(8,128)(2,1)S(1)}, u32[]{:S(2)}, u32[]{:S(2)}) %collective-permute-start.11) | collective-permute-done | bytes 819232 | tf_op jit(solution)/shard_map/ppermute | solution.py:109
  165.3 12.8 %collective-permute-done.12 = bf16[640,640]{1,0:T(8,128)(2,1)S(1)} collective-permute-done((bf16[640,640]{1,0:T(8,128)(2,1)S(1)}, bf16[640,640]{1,0:T(8,128)(2,1)S(1)}, u32[]{:S(2)}, u32[]{:S(2)}) %collective-permute-start.12) | collective-permute-done | bytes 819232 | tf_op jit(solution)/shard_map/ppermute | solution.py:109
  179.3 1.2 maximum_select_fusion
  (57 shorter events, 14.0 us)
Async XLA Ops:
  0.0 69.5 %collective-permute-start = (bf16[384,640]{1,0:T(8,128)(2,1)}, bf16[384,640]{1,0:T(8,128)(2,1)S(1)}, u32[]{:S(2)}, u32[]{:S(2)}) collective-permute-start(bf16[384,640]{1,0:T(8,128)(2,1)} %param.8), channel_id=1, source_target_pairs={{0,4},{4,8},{8,12},{1,5},{5,9},{9,13},{2,6},{6,10},{10,14},{3,7},{... | collective-permute-start | bytes 1474568 | tf_op jit(solution)/shard_map/ppermute | solution.py:15
  5.0 64.5 %collective-permute-start.1 = (bf16[384,640]{1,0:T(8,128)(2,1)}, bf16[384,640]{1,0:T(8,128)(2,1)}, u32[]{:S(2)}, u32[]{:S(2)}) collective-permute-start(bf16[384,640]{1,0:T(8,128)(2,1)} %param.8), channel_id=1, source_target_pairs={{4,0},{8,4},{12,8},{5,1},{9,5},{13,9},{6,2},{10,6},{14,10},{7,3},{... | collective-permute-start | bytes 1474568 | tf_op jit(solution)/shard_map/ppermute | solution.py:15
  6.3 65.6 %collective-permute-start.2 = (bf16[384,640]{1,0:T(8,128)(2,1)}, bf16[384,640]{1,0:T(8,128)(2,1)S(1)}, u32[]{:S(2)}, u32[]{:S(2)}) collective-permute-start(bf16[384,640]{1,0:T(8,128)(2,1)} %param.9), channel_id=1, source_target_pairs={{0,4},{4,8},{8,12},{1,5},{5,9},{9,13},{2,6},{6,10},{10,14},{3,7},{... | collective-permute-start | bytes 1474568 | tf_op jit(solution)/shard_map/ppermute | solution.py:15
  10.8 61.0 %collective-permute-start.3 = (bf16[384,640]{1,0:T(8,128)(2,1)}, bf16[384,640]{1,0:T(8,128)(2,1)}, u32[]{:S(2)}, u32[]{:S(2)}) collective-permute-start(bf16[384,640]{1,0:T(8,128)(2,1)} %param.9), channel_id=1, source_target_pairs={{4,0},{8,4},{12,8},{5,1},{9,5},{13,9},{6,2},{10,6},{14,10},{7,3},{... | collective-permute-start | bytes 1474568 | tf_op jit(solution)/shard_map/ppermute | solution.py:15
  12.1 51.8 %collective-permute-start.4 = (s32[384]{0:T(512)}, s32[384]{0:T(512)S(1)}, u32[]{:S(2)}, u32[]{:S(2)}) collective-permute-start(s32[384]{0:T(512)} %param.12), channel_id=1, source_target_pairs={{0,4},{4,8},{8,12},{1,5},{5,9},{9,13},{2,6},{6,10},{10,14},{3,7},{... | collective-permute-start | bytes 4616 | tf_op jit(solution)/shard_map/ppermute | solution.py:15
  16.7 47.0 %copy-start.6 = (s32[3]{0:T(128)S(1)}, s32[3]{0:T(128)}, u32[]{:S(2)}) copy-start(s32[3]{0:T(128)} %constant.86) | copy-start | bytes 40
  16.7 47.0 %copy-start.5 = (s32[4,27]{1,0:T(4,128)S(1)}, s32[4,27]{1,0:T(4,128)}, u32[]{:S(2)}) copy-start(s32[4,27]{1,0:T(4,128)} %param.11) | copy-start | bytes 1300
  16.7 47.2 %copy-start.3 = (s32[384]{0:T(512)S(1)}, s32[384]{0:T(512)}, u32[]{:S(2)}) copy-start(s32[384]{0:T(512)} %param.12) | copy-start | bytes 4612
  16.7 52.8 %copy-start.1 = (bf16[384,640]{1,0:T(8,128)(2,1)S(1)}, bf16[384,640]{1,0:T(8,128)(2,1)}, u32[]{:S(2)}) copy-start(bf16[384,640]{1,0:T(8,128)(2,1)} %param.8) | copy-start | bytes 1474564
  64.0 5.5 %collective-permute-start.5 = (s32[384]{0:T(512)S(1)}, s32[384]{0:T(512)S(1)}, u32[]{:S(2)}, u32[]{:S(2)}) collective-permute-start(s32[384]{0:T(512)S(1)} %copy-done.3), channel_id=1, source_target_pairs={{4,0},{8,4},{12,8},{5,1},{9,5},{13,9},{6,2},{10,6},{14,10},{7,3},{... | collective-permute-start | bytes 4616 | tf_op jit(solution)/shard_map/ppermute | solution.py:15
  71.9 0.8 copy-start.2
  74.2 2.2 %copy-start = (bf16[3,384,640]{2,1,0:T(8,128)(2,1)S(1)}, bf16[3,384,640]{2,1,0:T(8,128)(2,1)}, u32[]{:S(2)}) copy-start(bf16[3,384,640]{2,1,0:T(8,128)(2,1)} %pad_maximum_fusion.1) | copy-start | bytes 4423684
  74.2 2.2 %copy-start.4 = (bf16[384,640]{1,0:T(8,128)(2,1)S(1)}, bf16[384,640]{1,0:T(8,128)(2,1)}, u32[]{:S(2)}) copy-start(bf16[384,640]{1,0:T(8,128)(2,1)} %param.7) | copy-start | bytes 1474564
  78.9 47.1 %collective-permute-start.9 = (bf16[640,640]{1,0:T(8,128)(2,1)S(1)}, bf16[640,640]{1,0:T(8,128)(2,1)S(1)}, u32[]{:S(2)}, u32[]{:S(2)}) collective-permute-start(bf16[640,640]{1,0:T(8,128)(2,1)S(1)} %all_gather.12), channel_id=1, source_target_pairs={{0,16},{16,0},{1,17},{17,1},{2,18},{18,2},{3,19},{19,3},{4,20},{20... | collective-permute-start | bytes 2457608 | tf_op jit(solution)/shard_map/ppermute | solution.py:83
  87.4 39.2 %collective-permute-start.6 = (bf16[384,640]{0,1:T(8,128)(2,1)S(1)}, bf16[384,640]{0,1:T(8,128)(2,1)S(1)}, u32[]{:S(2)}, u32[]{:S(2)}) collective-permute-start(bf16[384,640]{0,1:T(8,128)(2,1)S(1)} %fusion.24), channel_id=1, source_target_pairs={{0,3},{1,0},{2,1},{3,2},{4,7},{5,4},{6,5},{7,6},{8,11},{9,8},{10,9... | collective-permute-start | bytes 1474568 | tf_op jit(solution)/shard_map/ppermute | solution.py:115
  87.4 39.1 %collective-permute-start.7 = (bf16[384,640]{0,1:T(8,128)(2,1)S(1)}, bf16[384,640]{0,1:T(8,128)(2,1)S(1)}, u32[]{:S(2)}, u32[]{:S(2)}) collective-permute-start(bf16[384,640]{0,1:T(8,128)(2,1)S(1)} %fusion.24), channel_id=1, source_target_pairs={{0,2},{1,3},{2,0},{3,1},{4,6},{5,7},{6,4},{7,5},{8,10},{9,11},{10,... | collective-permute-start | bytes 1474568 | tf_op jit(solution)/shard_map/ppermute | solution.py:115
  89.0 37.6 %collective-permute-start.8 = (bf16[384,640]{0,1:T(8,128)(2,1)S(1)}, bf16[384,640]{0,1:T(8,128)(2,1)S(1)}, u32[]{:S(2)}, u32[]{:S(2)}) collective-permute-start(bf16[384,640]{0,1:T(8,128)(2,1)S(1)} %fusion.24), channel_id=1, source_target_pairs={{0,1},{1,2},{2,3},{3,0},{4,5},{5,6},{6,7},{7,4},{8,9},{9,10},{10,1... | collective-permute-start | bytes 1474568 | tf_op jit(solution)/shard_map/ppermute | solution.py:115
  126.0 18.4 %collective-permute-start.10 = (bf16[640,640]{1,0:T(8,128)(2,1)S(1)}, bf16[640,640]{1,0:T(8,128)(2,1)S(1)}, u32[]{:S(2)}, u32[]{:S(2)}) collective-permute-start(bf16[640,640]{1,0:T(8,128)(2,1)S(1)} %all_gather.13), channel_id=1, source_target_pairs={{0,16},{16,0},{1,17},{17,1},{2,18},{18,2},{3,19},{19,3},{4,20},{20... | collective-permute-start | bytes 2457608 | tf_op jit(solution)/shard_map/ppermute | solution.py:109
  144.5 18.4 %collective-permute-start.11 = (bf16[640,640]{1,0:T(8,128)(2,1)S(1)}, bf16[640,640]{1,0:T(8,128)(2,1)S(1)}, u32[]{:S(2)}, u32[]{:S(2)}) collective-permute-start(bf16[640,640]{1,0:T(8,128)(2,1)S(1)} %all_gather.14), channel_id=1, source_target_pairs={{0,16},{16,0},{1,17},{17,1},{2,18},{18,2},{3,19},{19,3},{4,20},{20... | collective-permute-start | bytes 2457608 | tf_op jit(solution)/shard_map/ppermute | solution.py:109
  162.9 15.2 %collective-permute-start.12 = (bf16[640,640]{1,0:T(8,128)(2,1)S(1)}, bf16[640,640]{1,0:T(8,128)(2,1)S(1)}, u32[]{:S(2)}, u32[]{:S(2)}) collective-permute-start(bf16[640,640]{1,0:T(8,128)(2,1)S(1)} %all_gather.15), channel_id=1, source_target_pairs={{0,16},{16,0},{1,17},{17,1},{2,18},{18,2},{3,19},{19,3},{4,20},{20... | collective-permute-start | bytes 2457608 | tf_op jit(solution)/shard_map/ppermute | solution.py:109
where the time goes:
time: 181 us
  blocking collectives  82.5 us (46%)
  waiting for transfers between devices  49.9 us (28%)
  starting transfers between devices  22.8 us (13%)
  matrix products  14.3 us (8%)
  other arithmetic  8.06 us (4%)
  local copies, waits for them, and re-layouts  2.52 us (1%)
    all_gather x4, blocking collectives, on_device(): lax.all_gather(own_half[first:last], 'seq', axis=0, tiled=True)  82.5 us
    ppermute x3, waiting for transfers between devices, on_device(): crossed.append(lax.ppermute(gathered[index], 'rep', [(0, 1), (1, 0)]))  45.9 us
    ppermute x6, starting transfers between devices, from_behind(): return lax.ppermute(value, axis, pairs)  18 us
    dot_general x5, matrix products, attend_head(): lax.dot_general(query_head, key_head, (((1,), (1,)), ((), ())), preferred...  4.69 us
    dot_general x5, matrix products, attend_head(): jnp.dot(weights, value_head, preferred_element_type=jnp.float32)  4.59 us
    ppermute x6, waiting for transfers between devices, from_behind(): return lax.ppermute(value, axis, pairs)  4.04 us
  transfers between devices with their start and end apart: 13, of which 4 were waited for; matrix products, arithmetic and copies ran while one was open for 9% of the time, Pallas kernels for 0%

commit v1 on v0

--- a/solution.py
+++ b/solution.py
@@ -7,6 +7,28 @@
 HD = 128
 TGH = 4
 TGW = 7
+
+
+def in_order(tiles, dim):
+    lengths = list(tiles.shape[1:])
+    lengths[dim] *= tiles.shape[0]
+    return jnp.moveaxis(tiles, 0, dim).reshape(lengths)
+
+
+def collect(shard, axis, dim):
+    size = lax.axis_size(axis)
+    pairs = [(i, (i + 1) % size) for i in range(size)]
+    back = [(b, a) for a, b in pairs]
+    lower, upper = ([], [])
+    for step in range(size - 1):
+        if step % 2 == 0:
+            lower.append(lax.ppermute(lower[-1] if lower else shard, axis, pairs))
+        else:
+            upper.append(lax.ppermute(upper[-1] if upper else shard, axis, back))
+    blocks = jnp.stack([*lower[::-1], shard, *upper])
+    shift = lax.axis_index(axis) - len(lower)
+    blocks = blocks[(jnp.arange(size) - shift) % size]
+    return in_order(blocks, dim)
 
 
 def from_behind(value, axis, by):
@@ -55,10 +77,7 @@
     block_rows = out_weight.shape[0]
     own_half = lax.dynamic_slice_in_dim(out_weight, rep_position * half_width, half_width, axis=1)
     row_chunks = chunk_bounds(block_rows)
-    gathered = [
-        lax.all_gather(own_half[first:last], "seq", axis=0, tiled=True)
-        for first, last in row_chunks
-    ]
+    gathered = [collect(own_half[first:last], "seq", 0) for first, last in row_chunks]
     key_list = [keys]
     value_list = [values]
     clip_list = [clip_ids]

time: 181 us -> 157 us (0.87)
  blocking collectives: 82.5 us -> 0 us
  waiting for transfers between devices: 49.9 us -> 77 us
  starting transfers between devices: 22.8 us -> 38.5 us
  other arithmetic: 8.06 us -> 13.7 us
  local copies, waits for them, and re-layouts: 2.52 us -> 7.45 us
  matrix products: 14.3 us -> 19.2 us
    all_gather x4 -> x0, blocking collectives: 82.5 us -> none  [on_device(): lax.all_gather(own_half[first:last], 'seq', axis=0, tiled=True)]
    ppermute x0 -> x12, waiting for transfers between devices: none -> 28.7 us  [the longest x8 25.1 us: collect(): lower.append(lax.ppermute(lower[-1] if lower else shard, axis, pairs))]
    ppermute x0 -> x12, starting transfers between devices: none -> 18.6 us  [the longest x4 9.72 us: collect(): upper.append(lax.ppermute(upper[-1] if upper else shard, axis, back))]
    ppermute x3, waiting for transfers between devices: 45.9 us -> 37 us  [on_device(): crossed.append(lax.ppermute(gathered[index], 'rep', [(0, 1), (1, 0)]))]
    ppermute x6, waiting for transfers between devices: 4.04 us -> 11.3 us  [from_behind(): return lax.ppermute(value, axis, pairs)]
    another operation x0 -> x4, other arithmetic: none -> 3.77 us  [collect(): blocks = jnp.stack([*lower[::-1], shard, *upper])]
    gather x0 -> x4, local copies, waits for them, and re-layouts: none -> 3.63 us  [collect(): blocks = blocks[(jnp.arange(size) - shift) % size]]
    dot_general x5, matrix products: 4.59 us -> 7.77 us  [attend_head(): jnp.dot(weights, value_head, preferred_element_type=jnp.float32)]
  transfers between devices with their start and end apart: 13 -> 25, of which waited for: 4 -> 10; matrix products, arithmetic and copies ran while one was open for 9% -> 23% of each run, Pallas kernels for 0% -> 0%
where the time goes in v1:
time: 157 us; the launch traced here: 156 us
  waiting for transfers between devices  77 us (49%)
  starting transfers between devices  38.5 us (25%)
  matrix products  19.2 us (12%)
  other arithmetic  13.7 us (9%)
  local copies, waits for them, and re-layouts  7.45 us (5%)
    ppermute x3, waiting for transfers between devices, on_device(): crossed.append(lax.ppermute(gathered[index], 'rep', [(0, 1), (1, 0)]))  37 us
    ppermute x8, waiting for transfers between devices, collect(): lower.append(lax.ppermute(lower[-1] if lower else shard, axis, pairs))  25.1 us
    ppermute x6, starting transfers between devices, from_behind(): return lax.ppermute(value, axis, pairs)  15.2 us
    ppermute x6, waiting for transfers between devices, from_behind(): return lax.ppermute(value, axis, pairs)  11.3 us
    ppermute x4, starting transfers between devices, collect(): upper.append(lax.ppermute(upper[-1] if upper else shard, axis, back))  9.72 us
    ppermute x8, starting transfers between devices, collect(): lower.append(lax.ppermute(lower[-1] if lower else shard, axis, pairs))  8.89 us
    dot_general x5, matrix products, attend_head(): jnp.dot(weights, value_head, preferred_element_type=jnp.float32)  7.77 us
    dot_general x5, matrix products, attend_head(): lax.dot_general(query_head, key_head, (((1,), (1,)), ((), ())), preferred...  4.08 us
  transfers between devices with their start and end apart: 25, of which 10 were waited for; matrix products, arithmetic and copies ran while one was open for 23% of the time, Pallas kernels for 0%

profile of v1, /device:TPU:0, one launch (start us, length us, event | category | flops | bytes accessed | tf_op | source)
XLA Modules:
  0.0 156.1 jit_solution(1515452253918346759)
XLA Ops:
  0.0 2.0 %fusion.51 = (bf16[160,640]{1,0:T(8,128)(2,1)}, bf16[160,640]{1,0:T(8,128)(2,1)S(1)}, bf16[160,640]{1,0:T(8,128)(2,1)S(1)}, bf16[160,640]{1,0:T(8,128)(2,1)S(1)}) fusion(bf16[640,1280]{1,0:T(8,128)(2,1)} %param.10, s32[]{:T(128)S(6)} %add.96, s32[]{:T(128)S(6)} %select_n.189, s32[]{:T(128)S(6)} %add.97, s32[]{:T(128)S(6)} %add.98), kind=kLoop, calls=%fused_computation.102 | loop fusion | bytes 1638416 | tf_op jit(solution)/shard_map/slice | solution.py:80
  2.0 3.0 %collective-permute-start = (bf16[160,640]{1,0:T(8,128)(2,1)S(1)}, bf16[160,640]{1,0:T(8,128)(2,1)S(1)}, u32[]{:S(2)}, u32[]{:S(2)}) collective-permute-start(bf16[160,640]{1,0:T(8,128)(2,1)S(1)} %get-tuple-element.40), channel_id=1, source_target_pairs={{0,4},{4,8},{8,12},{12,0},{1,5},{5,9},{9,13},{13,1},{2,6},{6,10},{... | collective-permute-start | bytes 614408 | tf_op jit(solution)/shard_map/ppermute | solution.py:25
  5.0 2.0 %collective-permute-start.2 = (bf16[160,640]{1,0:T(8,128)(2,1)S(1)}, bf16[160,640]{1,0:T(8,128)(2,1)S(1)}, u32[]{:S(2)}, u32[]{:S(2)}) collective-permute-start(bf16[160,640]{1,0:T(8,128)(2,1)S(1)} %get-tuple-element.40), channel_id=1, source_target_pairs={{4,0},{8,4},{12,8},{0,12},{5,1},{9,5},{13,9},{1,13},{6,2},{10,6},{... | collective-permute-start | bytes 614408 | tf_op jit(solution)/shard_map/ppermute | solution.py:27
  8.3 5.4 %collective-permute-start.3 = (bf16[384,640]{1,0:T(8,128)(2,1)}, bf16[384,640]{1,0:T(8,128)(2,1)}, u32[]{:S(2)}, u32[]{:S(2)}) collective-permute-start(bf16[384,640]{1,0:T(8,128)(2,1)} %param.8), channel_id=1, source_target_pairs={{0,4},{4,8},{8,12},{1,5},{5,9},{9,13},{2,6},{6,10},{10,14},{3,7},{... | collective-permute-start | bytes 1474568 | tf_op jit(solution)/shard_map/ppermute | solution.py:37
  17.2 7.2 %collective-permute-done.7 = s32[384]{0:T(512)S(1)} collective-permute-done((s32[384]{0:T(512)}, s32[384]{0:T(512)S(1)}, u32[]{:S(2)}, u32[]{:S(2)}) %collective-permute-start.7) | collective-permute-done | bytes 1568 | tf_op jit(solution)/shard_map/ppermute | solution.py:37
  26.5 4.1 %collective-permute-done.8 = s32[384]{0:T(512)S(1)} collective-permute-done((s32[384]{0:T(512)}, s32[384]{0:T(512)S(1)}, u32[]{:S(2)}, u32[]{:S(2)}) %collective-permute-start.8) | collective-permute-done | bytes 1568 | tf_op jit(solution)/shard_map/ppermute | solution.py:37
  30.6 4.7 %collective-permute-start.5 = (bf16[384,640]{1,0:T(8,128)(2,1)}, bf16[384,640]{1,0:T(8,128)(2,1)}, u32[]{:S(2)}, u32[]{:S(2)}) collective-permute-start(bf16[384,640]{1,0:T(8,128)(2,1)} %param.9), channel_id=1, source_target_pairs={{0,4},{4,8},{8,12},{1,5},{5,9},{9,13},{2,6},{6,10},{10,14},{3,7},{... | collective-permute-start | bytes 1474568 | tf_op jit(solution)/shard_map/ppermute | solution.py:37
  36.6 2.7 %collective-permute-start.1 = (bf16[160,640]{1,0:T(8,128)(2,1)S(1)}, bf16[160,640]{1,0:T(8,128)(2,1)S(1)}, u32[]{:S(2)}, u32[]{:S(2)}) collective-permute-start(bf16[160,640]{1,0:T(8,128)(2,1)S(1)} %collective-permute-done), channel_id=1, source_target_pairs={{0,4},{4,8},{8,12},{12,0},{1,5},{5,9},{9,13},{13,1},{2,6},{6,10},{... | collective-permute-start | bytes 614408 | tf_op jit(solution)/shard_map/ppermute | solution.py:25
  39.3 14.2 %collective-permute-done.1 = bf16[160,640]{1,0:T(8,128)(2,1)S(1)} collective-permute-done((bf16[160,640]{1,0:T(8,128)(2,1)S(1)}, bf16[160,640]{1,0:T(8,128)(2,1)S(1)}, u32[]{:S(2)}, u32[]{:S(2)}) %collective-permute-start.1) | collective-permute-done | bytes 204832 | tf_op jit(solution)/shard_map/ppermute | solution.py:25
  55.2 3.8 %collective-permute-start.14 = (bf16[160,640]{1,0:T(8,128)(2,1)}, bf16[160,640]{1,0:T(8,128)(2,1)}, u32[]{:S(2)}, u32[]{:S(2)}) collective-permute-start(bf16[160,640]{1,0:T(8,128)(2,1)} %get-tuple-element.38), channel_id=1, source_target_pairs={{4,0},{8,4},{12,8},{0,12},{5,1},{9,5},{13,9},{1,13},{6,2},{10,6},{... | collective-permute-start | bytes 614408 | tf_op jit(solution)/shard_map/ppermute | solution.py:27
  60.6 3.9 %collective-permute-start.18 = (bf16[160,640]{1,0:T(8,128)(2,1)S(1)}, bf16[160,640]{1,0:T(8,128)(2,1)}, u32[]{:S(2)}, u32[]{:S(2)}) collective-permute-start(bf16[160,640]{1,0:T(8,128)(2,1)S(1)} %get-tuple-element.39), channel_id=1, source_target_pairs={{4,0},{8,4},{12,8},{0,12},{5,1},{9,5},{13,9},{1,13},{6,2},{10,6},{... | collective-permute-start | bytes 614408 | tf_op jit(solution)/shard_map/ppermute | solution.py:27
  70.0 1.6 %collective-permute-start.15 = (bf16[640,640]{1,0:T(8,128)(2,1)}, bf16[640,640]{1,0:T(8,128)(2,1)S(1)}, u32[]{:S(2)}, u32[]{:S(2)}) collective-permute-start(bf16[640,640]{1,0:T(8,128)(2,1)} %bitcast.7), channel_id=1, source_target_pairs={{0,16},{16,0},{1,17},{17,1},{2,18},{18,2},{3,19},{19,3},{4,20},{20... | collective-permute-start | bytes 2457608 | tf_op jit(solution)/shard_map/ppermute | solution.py:102
  71.6 2.2 %fusion.20 = (f32[384]{0:T(512)S(1)}, f32[384]{0:T(512)S(1)}, f32[384]{0:T(512)S(1)}, f32[384]{0:T(512)S(1)}, f32[384]{0:T(512)S(1)}) fusion(f32[384,1152]{0,1:T(8,128)S(1)} %get-tuple-element.43, f32[384]{0:T(512)S(1)} %get-tuple-element.42, s32[384]{0:T(512)S(1)} %copy-done.4, s32[1152]{0:T(1024)S(1)} %eq.94, pred[1152]{0:T(1024)(128)(4,1)S(1)} %and.70, ...), kind=kLoop, calls=%fused_computation.46 | loop fusion | flops 7518336 | bytes 8870016 | tf_op jit(solution)/shard_map/reduce_sum | solution.py:59
  84.2 5.5 %collective-permute-done.20 = bf16[160,640]{1,0:T(8,128)(2,1)} collective-permute-done((bf16[160,640]{1,0:T(8,128)(2,1)S(1)}, bf16[160,640]{1,0:T(8,128)(2,1)}, u32[]{:S(2)}, u32[]{:S(2)}) %collective-permute-start.20) | collective-permute-done | bytes 204832 | tf_op jit(solution)/shard_map/ppermute | solution.py:25
  89.8 2.1 %collective-permute-done.13 = bf16[160,640]{1,0:T(8,128)(2,1)S(1)} collective-permute-done((bf16[160,640]{1,0:T(8,128)(2,1)}, bf16[160,640]{1,0:T(8,128)(2,1)S(1)}, u32[]{:S(2)}, u32[]{:S(2)}) %collective-permute-start.13) | collective-permute-done | bytes 204832 | tf_op jit(solution)/shard_map/ppermute | solution.py:25
  91.9 3.2 %collective-permute-done.17 = bf16[160,640]{1,0:T(8,128)(2,1)S(1)} collective-permute-done((bf16[160,640]{1,0:T(8,128)(2,1)}, bf16[160,640]{1,0:T(8,128)(2,1)S(1)}, u32[]{:S(2)}, u32[]{:S(2)}) %collective-permute-start.17) | collective-permute-done | bytes 204832 | tf_op jit(solution)/shard_map/ppermute | solution.py:25
  95.1 2.0 %collective-permute-start.21 = (bf16[160,640]{1,0:T(8,128)(2,1)}, bf16[160,640]{1,0:T(8,128)(2,1)}, u32[]{:S(2)}, u32[]{:S(2)}) collective-permute-start(bf16[160,640]{1,0:T(8,128)(2,1)} %collective-permute-done.20), channel_id=1, source_target_pairs={{0,4},{4,8},{8,12},{12,0},{1,5},{5,9},{9,13},{13,1},{2,6},{6,10},{... | collective-permute-start | bytes 614408 | tf_op jit(solution)/shard_map/ppermute | solution.py:25
  100.9 3.6 %collective-permute-done.22 = bf16[160,640]{1,0:T(8,128)(2,1)S(1)} collective-permute-done((bf16[160,640]{1,0:T(8,128)(2,1)S(1)}, bf16[160,640]{1,0:T(8,128)(2,1)S(1)}, u32[]{:S(2)}, u32[]{:S(2)}) %collective-permute-start.22) | collective-permute-done | bytes 204832 | tf_op jit(solution)/shard_map/ppermute | solution.py:27
  107.2 1.8 %select_select_fusion.3 = (bf16[384,640]{0,1:T(8,128)(2,1)S(1)}, bf16[384,640]{0,1:T(8,128)(2,1)S(1)}, bf16[384,640]{0,1:T(8,128)(2,1)S(1)}, bf16[384,640]{0,1:T(8,128)(2,1)S(1)}) fusion(bf16[384,640]{0,1:T(8,128)(2,1)} %collective-permute-done.9, bf16[384,640]{0,1:T(8,128)(2,1)} %collective-permute-done.10, bf16[384,640]{0,1:T(8,128)(2,1)} %collective-permute-done.11, ...), kind=kLoop, calls=%fused_computation.65 | loop fusion | flops 2949120 | bytes 3932172 | tf_op jit(solution)/shard_map/jit(_where)/select_n | solution.py:139
  109.2 13.7 %collective-permute-done.19 = bf16[640,640]{1,0:T(8,128)(2,1)} collective-permute-done((bf16[640,640]{1,0:T(8,128)(2,1)S(1)}, bf16[640,640]{1,0:T(8,128)(2,1)}, u32[]{:S(2)}, u32[]{:S(2)}) %collective-permute-start.19) | collective-permute-done | bytes 819232 | tf_op jit(solution)/shard_map/ppermute | solution.py:128
  123.7 1.8 %convolution_bitcast_fusion = f32[384,640]{1,0:T(8,128)S(1)} fusion(bf16[4,160,640]{2,1,0:T(8,128)(2,1)} %gather_fusion, bf16[384,4,640]{0,2,1:T(8,128)(2,1)S(1)} %bitcast.77), kind=kOutput, calls=%fused_computation.39 | convolution fusion | flops 314572800 | bytes 2293760 | tf_op jit(solution)/shard_map/dot_general | solution.py:148
  126.1 1.8 %fusion.59 = f32[384,640]{1,0:T(8,128)S(1)} fusion(bf16[384,640]{0,1:T(8,128)(2,1)S(1)} %bitcast.80, bf16[640,640]{1,0:T(8,128)(2,1)} %collective-permute-done.19), kind=kOutput, calls=%fused_computation.110 | convolution fusion | flops 314572800 | bytes 2293760 | tf_op jit(solution)/shard_map/dot_general | solution.py:149
  127.9 13.4 %collective-permute-done.23 = bf16[640,640]{1,0:T(8,128)(2,1)S(1)} collective-permute-done((bf16[640,640]{1,0:T(8,128)(2,1)S(1)}, bf16[640,640]{1,0:T(8,128)(2,1)S(1)}, u32[]{:S(2)}, u32[]{:S(2)}) %collective-permute-start.23) | collective-permute-done | bytes 819232 | tf_op jit(solution)/shard_map/ppermute | solution.py:128
  143.8 9.8 %collective-permute-done.24 = bf16[640,640]{1,0:T(8,128)(2,1)S(1)} collective-permute-done((bf16[640,640]{1,0:T(8,128)(2,1)S(1)}, bf16[640,640]{1,0:T(8,128)(2,1)S(1)}, u32[]{:S(2)}, u32[]{:S(2)}) %collective-permute-start.24) | collective-permute-done | bytes 819232 | tf_op jit(solution)/shard_map/ppermute | solution.py:128
  (85 shorter events, 40.2 us)
Async XLA Ops:
  2.0 33.3 %collective-permute-start = (bf16[160,640]{1,0:T(8,128)(2,1)S(1)}, bf16[160,640]{1,0:T(8,128)(2,1)S(1)}, u32[]{:S(2)}, u32[]{:S(2)}) collective-permute-start(bf16[160,640]{1,0:T(8,128)(2,1)S(1)} %get-tuple-element.40), channel_id=1, source_target_pairs={{0,4},{4,8},{8,12},{12,0},{1,5},{5,9},{9,13},{13,1},{2,6},{6,10},{... | collective-permute-start | bytes 614408 | tf_op jit(solution)/shard_map/ppermute | solution.py:25
  5.0 31.6 %collective-permute-start.2 = (bf16[160,640]{1,0:T(8,128)(2,1)S(1)}, bf16[160,640]{1,0:T(8,128)(2,1)S(1)}, u32[]{:S(2)}, u32[]{:S(2)}) collective-permute-start(bf16[160,640]{1,0:T(8,128)(2,1)S(1)} %get-tuple-element.40), channel_id=1, source_target_pairs={{4,0},{8,4},{12,8},{0,12},{5,1},{9,5},{13,9},{1,13},{6,2},{10,6},{... | collective-permute-start | bytes 614408 | tf_op jit(solution)/shard_map/ppermute | solution.py:27
  7.0 48.2 %collective-permute-start.4 = (bf16[384,640]{1,0:T(8,128)(2,1)}, bf16[384,640]{1,0:T(8,128)(2,1)}, u32[]{:S(2)}, u32[]{:S(2)}) collective-permute-start(bf16[384,640]{1,0:T(8,128)(2,1)} %param.8), channel_id=1, source_target_pairs={{4,0},{8,4},{12,8},{5,1},{9,5},{13,9},{6,2},{10,6},{14,10},{7,3},{... | collective-permute-start | bytes 1474568 | tf_op jit(solution)/shard_map/ppermute | solution.py:37
  8.3 50.7 %collective-permute-start.3 = (bf16[384,640]{1,0:T(8,128)(2,1)}, bf16[384,640]{1,0:T(8,128)(2,1)}, u32[]{:S(2)}, u32[]{:S(2)}) collective-permute-start(bf16[384,640]{1,0:T(8,128)(2,1)} %param.8), channel_id=1, source_target_pairs={{0,4},{4,8},{8,12},{1,5},{5,9},{9,13},{2,6},{6,10},{10,14},{3,7},{... | collective-permute-start | bytes 1474568 | tf_op jit(solution)/shard_map/ppermute | solution.py:37
  13.7 10.8 %collective-permute-start.7 = (s32[384]{0:T(512)}, s32[384]{0:T(512)S(1)}, u32[]{:S(2)}, u32[]{:S(2)}) collective-permute-start(s32[384]{0:T(512)} %param.12), channel_id=1, source_target_pairs={{0,4},{4,8},{8,12},{1,5},{5,9},{9,13},{2,6},{6,10},{10,14},{3,7},{... | collective-permute-start | bytes 4616 | tf_op jit(solution)/shard_map/ppermute | solution.py:37
  30.6 30.0 %collective-permute-start.5 = (bf16[384,640]{1,0:T(8,128)(2,1)}, bf16[384,640]{1,0:T(8,128)(2,1)}, u32[]{:S(2)}, u32[]{:S(2)}) collective-permute-start(bf16[384,640]{1,0:T(8,128)(2,1)} %param.9), channel_id=1, source_target_pairs={{0,4},{4,8},{8,12},{1,5},{5,9},{9,13},{2,6},{6,10},{10,14},{3,7},{... | collective-permute-start | bytes 1474568 | tf_op jit(solution)/shard_map/ppermute | solution.py:37
  35.3 29.2 %collective-permute-start.6 = (bf16[384,640]{1,0:T(8,128)(2,1)}, bf16[384,640]{1,0:T(8,128)(2,1)}, u32[]{:S(2)}, u32[]{:S(2)}) collective-permute-start(bf16[384,640]{1,0:T(8,128)(2,1)} %param.9), channel_id=1, source_target_pairs={{4,0},{8,4},{12,8},{5,1},{9,5},{13,9},{6,2},{10,6},{14,10},{7,3},{... | collective-permute-start | bytes 1474568 | tf_op jit(solution)/shard_map/ppermute | solution.py:37
  36.6 17.0 %collective-permute-start.1 = (bf16[160,640]{1,0:T(8,128)(2,1)S(1)}, bf16[160,640]{1,0:T(8,128)(2,1)S(1)}, u32[]{:S(2)}, u32[]{:S(2)}) collective-permute-start(bf16[160,640]{1,0:T(8,128)(2,1)S(1)} %collective-permute-done), channel_id=1, source_target_pairs={{0,4},{4,8},{8,12},{12,0},{1,5},{5,9},{9,13},{13,1},{2,6},{6,10},{... | collective-permute-start | bytes 614408 | tf_op jit(solution)/shard_map/ppermute | solution.py:25
  53.5 26.5 %collective-permute-start.12 = (bf16[160,640]{1,0:T(8,128)(2,1)}, bf16[160,640]{1,0:T(8,128)(2,1)}, u32[]{:S(2)}, u32[]{:S(2)}) collective-permute-start(bf16[160,640]{1,0:T(8,128)(2,1)} %get-tuple-element.38), channel_id=1, source_target_pairs={{0,4},{4,8},{8,12},{12,0},{1,5},{5,9},{9,13},{13,1},{2,6},{6,10},{... | collective-permute-start | bytes 614408 | tf_op jit(solution)/shard_map/ppermute | solution.py:25
  55.2 24.8 %collective-permute-start.14 = (bf16[160,640]{1,0:T(8,128)(2,1)}, bf16[160,640]{1,0:T(8,128)(2,1)}, u32[]{:S(2)}, u32[]{:S(2)}) collective-permute-start(bf16[160,640]{1,0:T(8,128)(2,1)} %get-tuple-element.38), channel_id=1, source_target_pairs={{4,0},{8,4},{12,8},{0,12},{5,1},{9,5},{13,9},{1,13},{6,2},{10,6},{... | collective-permute-start | bytes 614408 | tf_op jit(solution)/shard_map/ppermute | solution.py:27
  59.0 21.1 %collective-permute-start.16 = (bf16[160,640]{1,0:T(8,128)(2,1)S(1)}, bf16[160,640]{1,0:T(8,128)(2,1)}, u32[]{:S(2)}, u32[]{:S(2)}) collective-permute-start(bf16[160,640]{1,0:T(8,128)(2,1)S(1)} %get-tuple-element.39), channel_id=1, source_target_pairs={{0,4},{4,8},{8,12},{12,0},{1,5},{5,9},{9,13},{13,1},{2,6},{6,10},{... | collective-permute-start | bytes 614408 | tf_op jit(solution)/shard_map/ppermute | solution.py:25
  60.6 22.2 %collective-permute-start.18 = (bf16[160,640]{1,0:T(8,128)(2,1)S(1)}, bf16[160,640]{1,0:T(8,128)(2,1)}, u32[]{:S(2)}, u32[]{:S(2)}) collective-permute-start(bf16[160,640]{1,0:T(8,128)(2,1)S(1)} %get-tuple-element.39), channel_id=1, source_target_pairs={{4,0},{8,4},{12,8},{0,12},{5,1},{9,5},{13,9},{1,13},{6,2},{10,6},{... | collective-permute-start | bytes 614408 | tf_op jit(solution)/shard_map/ppermute | solution.py:27
  70.0 25.1 %collective-permute-start.15 = (bf16[640,640]{1,0:T(8,128)(2,1)}, bf16[640,640]{1,0:T(8,128)(2,1)S(1)}, u32[]{:S(2)}, u32[]{:S(2)}) collective-permute-start(bf16[640,640]{1,0:T(8,128)(2,1)} %bitcast.7), channel_id=1, source_target_pairs={{0,16},{16,0},{1,17},{17,1},{2,18},{18,2},{3,19},{19,3},{4,20},{20... | collective-permute-start | bytes 2457608 | tf_op jit(solution)/shard_map/ppermute | solution.py:102
  80.0 9.7 %collective-permute-start.20 = (bf16[160,640]{1,0:T(8,128)(2,1)S(1)}, bf16[160,640]{1,0:T(8,128)(2,1)}, u32[]{:S(2)}, u32[]{:S(2)}) collective-permute-start(bf16[160,640]{1,0:T(8,128)(2,1)S(1)} %get-tuple-element.41), channel_id=1, source_target_pairs={{0,4},{4,8},{8,12},{12,0},{1,5},{5,9},{9,13},{13,1},{2,6},{6,10},{... | collective-permute-start | bytes 614408 | tf_op jit(solution)/shard_map/ppermute | solution.py:25
  80.0 11.8 %collective-permute-start.13 = (bf16[160,640]{1,0:T(8,128)(2,1)}, bf16[160,640]{1,0:T(8,128)(2,1)S(1)}, u32[]{:S(2)}, u32[]{:S(2)}) collective-permute-start(bf16[160,640]{1,0:T(8,128)(2,1)} %collective-permute-done.12), channel_id=1, source_target_pairs={{0,4},{4,8},{8,12},{12,0},{1,5},{5,9},{9,13},{13,1},{2,6},{6,10},{... | collective-permute-start | bytes 614408 | tf_op jit(solution)/shard_map/ppermute | solution.py:25
  80.1 14.9 %collective-permute-start.17 = (bf16[160,640]{1,0:T(8,128)(2,1)}, bf16[160,640]{1,0:T(8,128)(2,1)S(1)}, u32[]{:S(2)}, u32[]{:S(2)}) collective-permute-start(bf16[160,640]{1,0:T(8,128)(2,1)} %collective-permute-done.16), channel_id=1, source_target_pairs={{0,4},{4,8},{8,12},{12,0},{1,5},{5,9},{9,13},{13,1},{2,6},{6,10},{... | collective-permute-start | bytes 614408 | tf_op jit(solution)/shard_map/ppermute | solution.py:25
  82.7 24.4 %collective-permute-start.10 = (bf16[384,640]{0,1:T(8,128)(2,1)}, bf16[384,640]{0,1:T(8,128)(2,1)}, u32[]{:S(2)}, u32[]{:S(2)}) collective-permute-start(bf16[384,640]{0,1:T(8,128)(2,1)} %fusion.25), channel_id=1, source_target_pairs={{0,2},{1,3},{2,0},{3,1},{4,6},{5,7},{6,4},{7,5},{8,10},{9,11},{10,... | collective-permute-start | bytes 1474568 | tf_op jit(solution)/shard_map/ppermute | solution.py:134
  89.8 17.4 %collective-permute-start.11 = (bf16[384,640]{0,1:T(8,128)(2,1)}, bf16[384,640]{0,1:T(8,128)(2,1)}, u32[]{:S(2)}, u32[]{:S(2)}) collective-permute-start(bf16[384,640]{0,1:T(8,128)(2,1)} %fusion.25), channel_id=1, source_target_pairs={{0,1},{1,2},{2,3},{3,0},{4,5},{5,6},{6,7},{7,4},{8,9},{9,10},{10,1... | collective-permute-start | bytes 1474568 | tf_op jit(solution)/shard_map/ppermute | solution.py:134
  91.9 15.3 %collective-permute-start.9 = (bf16[384,640]{0,1:T(8,128)(2,1)}, bf16[384,640]{0,1:T(8,128)(2,1)}, u32[]{:S(2)}, u32[]{:S(2)}) collective-permute-start(bf16[384,640]{0,1:T(8,128)(2,1)} %fusion.25), channel_id=1, source_target_pairs={{0,3},{1,0},{2,1},{3,2},{4,7},{5,4},{6,5},{7,6},{8,11},{9,8},{10,9... | collective-permute-start | bytes 1474568 | tf_op jit(solution)/shard_map/ppermute | solution.py:134
  95.0 9.5 %collective-permute-start.22 = (bf16[160,640]{1,0:T(8,128)(2,1)S(1)}, bf16[160,640]{1,0:T(8,128)(2,1)S(1)}, u32[]{:S(2)}, u32[]{:S(2)}) collective-permute-start(bf16[160,640]{1,0:T(8,128)(2,1)S(1)} %get-tuple-element.41), channel_id=1, source_target_pairs={{4,0},{8,4},{12,8},{0,12},{5,1},{9,5},{13,9},{1,13},{6,2},{10,6},{... | collective-permute-start | bytes 614408 | tf_op jit(solution)/shard_map/ppermute | solution.py:27
  95.1 10.0 %collective-permute-start.21 = (bf16[160,640]{1,0:T(8,128)(2,1)}, bf16[160,640]{1,0:T(8,128)(2,1)}, u32[]{:S(2)}, u32[]{:S(2)}) collective-permute-start(bf16[160,640]{1,0:T(8,128)(2,1)} %collective-permute-done.20), channel_id=1, source_target_pairs={{0,4},{4,8},{8,12},{12,0},{1,5},{5,9},{9,13},{13,1},{2,6},{6,10},{... | collective-permute-start | bytes 614408 | tf_op jit(solution)/shard_map/ppermute | solution.py:25
  104.5 18.4 %collective-permute-start.19 = (bf16[640,640]{1,0:T(8,128)(2,1)S(1)}, bf16[640,640]{1,0:T(8,128)(2,1)}, u32[]{:S(2)}, u32[]{:S(2)}) collective-permute-start(bf16[640,640]{1,0:T(8,128)(2,1)S(1)} %bitcast.84), channel_id=1, source_target_pairs={{0,16},{16,0},{1,17},{17,1},{2,18},{18,2},{3,19},{19,3},{4,20},{20... | collective-permute-start | bytes 2457608 | tf_op jit(solution)/shard_map/ppermute | solution.py:128
  122.9 18.4 %collective-permute-start.23 = (bf16[640,640]{1,0:T(8,128)(2,1)S(1)}, bf16[640,640]{1,0:T(8,128)(2,1)S(1)}, u32[]{:S(2)}, u32[]{:S(2)}) collective-permute-start(bf16[640,640]{1,0:T(8,128)(2,1)S(1)} %bitcast.88), channel_id=1, source_target_pairs={{0,16},{16,0},{1,17},{17,1},{2,18},{18,2},{3,19},{19,3},{4,20},{20... | collective-permute-start | bytes 2457608 | tf_op jit(solution)/shard_map/ppermute | solution.py:128
  141.3 12.3 %collective-permute-start.24 = (bf16[640,640]{1,0:T(8,128)(2,1)S(1)}, bf16[640,640]{1,0:T(8,128)(2,1)S(1)}, u32[]{:S(2)}, u32[]{:S(2)}) collective-permute-start(bf16[640,640]{1,0:T(8,128)(2,1)S(1)} %bitcast.86), channel_id=1, source_target_pairs={{0,16},{16,0},{1,17},{17,1},{2,18},{18,2},{3,19},{19,3},{4,20},{20... | collective-permute-start | bytes 2457608 | tf_op jit(solution)/shard_map/ppermute | solution.py:128
  (7 other events, 35.5 us)
